TPU v7x, 32 devices: a whole 2x2x4 slice. The times are simulated.
32 devices in a mesh: dp: 4 (over y, x), seq: 8 (over z, core).
Axes of the slice: x: 2, y: 2, z: 4, core: 2. Of those that a mesh axis runs over, the one named last changes fastest.
Arguments:
- asking_vectors_matrix: bfloat16 [4, 1024, 2048], P('dp', 'seq'), may hold values from -6 to 6
- matched_keys_matrix: bfloat16 [4, 1024, 2048], P('dp', 'seq'), may hold values from -6 to 6
- carried_vectors_matrix: bfloat16 [4, 1024, 2048], P('dp', 'seq'), may hold values from -6 to 6
- upstream_cotangent: bfloat16 [4, 1024, 2048], P('dp', 'seq'), may hold values from -6 to 6
- w_out: bfloat16 [2048, 2048], P('seq'), may hold values from -0.125 to 0.125
- panel_entry_offsets: int32 [4, 9], P('dp'), may hold values from 0 to 32, as said below
- rightward_panel_per_entry: int32 [4, 32], P('dp'), may hold values from 0 to 7, as said below
Outputs:
- layer_out: bfloat16 [4, 1024, 2048], P('dp', 'seq')
- q_grad: bfloat16 [4, 1024, 2048], P('dp', 'seq')
- k_grad: bfloat16 [4, 1024, 2048], P('dp', 'seq')
- v_grad: bfloat16 [4, 1024, 2048], P('dp', 'seq')
- w_out_grad: float32 [2048, 2048], P('seq')
Inputs may be any that keep to these rules, and one draw needn't show every extreme that they name: panel_entry_offsets[b, 0] is 0 and panel_entry_offsets never falls along a row; tile row r owns slots panel_entry_offsets[b, r] to panel_entry_offsets[b, r + 1] - 1, 1 to 8 of them, and its own tile r is among its blocks; in every subgraph one tile row holds all 8 tiles; panel_entry_offsets[b, 8], the used slots, lies between 16 and 32 and equals 32 for at least one subgraph. `rightward_panel_per_entry`: the slots of a tile row hold distinct column tiles in rising order; slots from panel_entry_offsets[b, 8] on hold arbitrary tile numbers that take no part.
All inputs are finite; a program needn't handle non-finite values.
Results may differ from a plain program's by a relative error of at most 0.034.
Values may be sent and summed in bfloat16 or wider, within the bound.
No kernel may reach another device: no remote copies, remote signals or barrier semaphores. Data moves between devices by JAX's collectives and lax.ppermute only.
A program may use at most 128 MiB of HBM per device.

v0:
```python
import math
import jax
import jax.numpy as jnp
from jax import lax
from jax.sharding import PartitionSpec as P

H = 16
HD = 128


def tile_mask(starts, columns, nodes):
    tile_count = starts.shape[0] - 1
    slot_count = columns.shape[0]
    tile_size = nodes // tile_count
    slot_index = jnp.arange(slot_count, dtype=jnp.int32)
    entry_row = jnp.sum((starts[1:][None, :] <= slot_index[:, None]).astype(jnp.int32), axis=1)
    tile_ids = jnp.arange(tile_count, dtype=jnp.int32)
    row_hot = (entry_row[:, None] == tile_ids[None, :]).astype(jnp.int32)
    col_hot = (columns[:, None] == tile_ids[None, :]).astype(jnp.int32)
    pairs = jnp.einsum("er,ec->rc", row_hot, col_hot) > 0
    full = jnp.broadcast_to(pairs[:, None, :, None], (tile_count, tile_size, tile_count, tile_size))
    return jnp.where(full.reshape(nodes, nodes), 0.0, -jnp.inf)


def attend(q, k, v, allowed):
    factor = 1.0 / math.sqrt(q.shape[-1])
    scores = jnp.dot(q, k.T, preferred_element_type=jnp.float32) * factor
    masked = scores + allowed
    row_max = jnp.max(masked, axis=1, keepdims=True)
    expd = jnp.exp(masked - row_max)
    row_total = jnp.sum(expd, axis=1, keepdims=True)
    weighted = jnp.dot(expd.astype(jnp.bfloat16), v, preferred_element_type=jnp.float32)
    attended = (weighted / row_total).astype(jnp.bfloat16)
    return (attended, expd, row_total)


def attend_back(q, k, v, g, attended, expd, row_total):
    factor = 1.0 / math.sqrt(q.shape[-1])
    prob = expd * (1.0 / row_total)
    prob_low = prob.astype(jnp.bfloat16)
    v_grad = jnp.dot(prob_low.T, g, preferred_element_type=jnp.float32)
    prob_grad = jnp.dot(g, v.T, preferred_element_type=jnp.float32)
    delta = jnp.sum(attended.astype(jnp.float32) * g.astype(jnp.float32), axis=1, keepdims=True)
    score_grad = (prob * (prob_grad - delta) * factor).astype(jnp.bfloat16)
    q_grad = jnp.dot(score_grad, k, preferred_element_type=jnp.float32)
    k_grad = jnp.dot(score_grad.T, q, preferred_element_type=jnp.float32)
    return (q_grad.astype(jnp.bfloat16), k_grad.astype(jnp.bfloat16), v_grad.astype(jnp.bfloat16))


def chip_layer_out(att_flat, w_out):
    n = lax.axis_size("seq")
    rows = att_flat.shape[0] // n
    chips = n // 2
    s = lax.axis_index("seq")
    core = s % 2
    z = s // 2
    sibling = [(i, i ^ 1) for i in range(n)]
    att_sib = lax.ppermute(att_flat, "seq", sibling)
    w_sib = lax.ppermute(w_out, "seq", sibling)

    def parity_rows(values):
        quads = values.reshape(chips, 2, rows, values.shape[1])
        return jnp.where(core == 0, quads[:, 0], quads[:, 1])

    att_chip = jnp.concatenate([parity_rows(att_flat), parity_rows(att_sib)], axis=2)
    w_chip = jnp.concatenate([w_out, w_sib], axis=0)
    chip_partial = lax.dot_general(
        att_chip, w_chip, (((2,), (0,)), ((), ())), preferred_element_type=jnp.float32
    )
    total = lax.dynamic_index_in_dim(chip_partial, z, 0, keepdims=False)
    sent = chip_partial.astype(jnp.bfloat16)
    for k in range(1, chips):
        pairs = [(i, (i // 2 + k) % chips * 2 + i % 2) for i in range(n)]
        piece = lax.dynamic_index_in_dim(sent, (z + k) % chips, 0, keepdims=False)
        total = total + lax.ppermute(piece, "seq", pairs).astype(jnp.float32)
    return total


def shards(
    asking_vectors_matrix,
    matched_keys_matrix,
    carried_vectors_matrix,
    upstream_cotangent,
    w_out,
    panel_entry_offsets,
    rightward_panel_per_entry,
):
    nodes_here = asking_vectors_matrix.shape[1]
    width = asking_vectors_matrix.shape[2]
    n_seq = lax.axis_size("seq")
    nodes = nodes_here * n_seq
    grad_here = upstream_cotangent[0]
    grad_full = lax.all_gather(grad_here, "seq", axis=0, tiled=True)
    groups = n_seq
    group_width = width // groups
    local_heads = group_width // HD

    def to_groups(values):
        return values.reshape(nodes_here, groups, group_width).transpose(1, 0, 2)

    stacked = jnp.stack(
        [
            to_groups(asking_vectors_matrix[0]),
            to_groups(matched_keys_matrix[0]),
            to_groups(carried_vectors_matrix[0]),
        ]
    )
    heads = lax.all_to_all(stacked, "seq", split_axis=1, concat_axis=1, tiled=True)
    heads = heads.reshape(3, nodes, group_width)
    allowed = tile_mask(panel_entry_offsets[0], rightward_panel_per_entry[0], nodes)

    def head_cols(values, h):
        return values[:, h * HD : (h + 1) * HD]

    fwd = [
        attend(head_cols(heads[0], h), head_cols(heads[1], h), head_cols(heads[2], h), allowed)
        for h in range(local_heads)
    ]
    att_flat = jnp.concatenate([f[0] for f in fwd], axis=1)
    layer_out = chip_layer_out(att_flat, w_out).astype(jnp.bfloat16)[None]
    g_flat = lax.dot_general(
        grad_full, w_out, (((1,), (1,)), ((), ())), preferred_element_type=jnp.float32
    ).astype(jnp.bfloat16)
    att_blocks = att_flat.reshape(n_seq, nodes_here, local_heads * HD)
    grad_blocks = grad_full.reshape(n_seq, nodes_here, width)
    terms = jnp.einsum(
        "bnf,bnk->bfk", att_blocks, grad_blocks, preferred_element_type=jnp.float32
    ).astype(jnp.bfloat16)
    w_rows = jnp.sum(terms.astype(jnp.float32), axis=0)
    w_rows = lax.psum(w_rows.astype(jnp.bfloat16), "dp").astype(jnp.float32)
    batch = asking_vectors_matrix.shape[0] * lax.axis_size("dp")
    w_out_grad = w_rows / batch
    bwd = [
        attend_back(
            head_cols(heads[0], h),
            head_cols(heads[1], h),
            head_cols(heads[2], h),
            head_cols(g_flat, h),
            fwd[h][0],
            fwd[h][1],
            fwd[h][2],
        )
        for h in range(local_heads)
    ]
    grads = jnp.stack(
        [
            jnp.concatenate([b[i] for b in bwd], axis=1).reshape(groups, nodes_here, group_width)
            for i in range(3)
        ]
    )
    back = lax.all_to_all(grads, "seq", split_axis=1, concat_axis=1, tiled=True)
    back = back.transpose(0, 2, 1, 3).reshape(3, 1, nodes_here, width)
    return (layer_out, back[0], back[1], back[2], w_out_grad)


def solution(mesh):
    return jax.shard_map(
        shards,
        mesh=mesh,
        in_specs=(
            P("dp", "seq", None),
            P("dp", "seq", None),
            P("dp", "seq", None),
            P("dp", "seq", None),
            P("seq", None),
            P("dp", None),
            P("dp", None),
        ),
        out_specs=(
            P("dp", "seq", None),
            P("dp", "seq", None),
            P("dp", "seq", None),
            P("dp", "seq", None),
            P("seq", None),
        ),
        check_vma=False,
    )
```

profile of v0, /device:TPU:10, one launch (start us, length us, event | category | flops | bytes accessed | tf_op | source)
XLA Modules:
  0.0 211.3 jit_solution(6985377320653367382)
XLA Ops:
  7.2 0.7 all-gather.3.cloned.1.call-update
  7.9 1.3 copy.72
  9.2 1.3 copy.73
  10.5 1.3 copy.74
  12.1 1.2 copy.75
  13.3 5.3 %all-to-all-start = ((bf16[3,8,128,256]{2,3,0,1:T(8,128)(2,1)}), bf16[3,8,128,256]{2,3,0,1:T(8,128)(2,1)S(1)}, u32[]{:S(2)}, u32[]{:S(2)}) async-start(bf16[3,8,128,256]{2,3,0,1:T(8,128)(2,1)} %copy.75), calls=%async_computation | async-start | bytes 3145728 | tf_op jit(solution)/shard_map/all_to_all | solution.py:108
  19.3 67.4 %all-to-all-done = bf16[3,8,128,256]{2,3,0,1:T(8,128)(2,1)S(1)} async-done(((bf16[3,8,128,256]{2,3,0,1:T(8,128)(2,1)}), bf16[3,8,128,256]{2,3,0,1:T(8,128)(2,1)S(1)}, u32[]{:S(2)}, u32[]{:S(2)}) %all-to-all-start) | async-done | bytes 1572896 | tf_op jit(solution)/shard_map/all_to_all | solution.py:108
  87.9 1.2 fusion.73
  89.1 0.6 fusion.2
  89.7 1.2 fusion.72
  91.1 0.6 fusion.4
  91.7 1.3 copy-done.2
  93.0 0.8 fusion.32
  93.9 3.9 %fusion.21 = bf16[1024,256]{0,1:T(8,128)(2,1)S(1)} fusion(bf16[256,2048]{1,0:T(8,128)(2,1)} %param.11, bf16[1,1024,2048]{2,1,0:T(8,128)(2,1)} %all-gather.3.cloned.1.call-done), kind=kOutput, calls=%fused_computation.32 | convolution fusion | flops 1074003968 | bytes 5767168 | tf_op jit(solution)/shard_map/dot_general | solution.py:121
  97.8 0.9 multiply_reduce_fusion.1
  98.7 1.2 multiply_convert_fusion.1
  99.9 0.5 convolution_convert_fusion.3
  100.4 0.8 convolution_convert_fusion.1
  101.2 0.8 copy-done.3
  102.1 1.2 multiply_convert_fusion
  103.3 0.5 convolution_convert_fusion.2
  103.8 0.8 convolution_convert_fusion
  104.6 1.1 fusion.31
  105.7 0.9 fusion.30
  106.7 1.0 fusion.67
  108.8 1.4 pad_maximum_fusion.1
  110.1 6.9 %all-to-all-start.1 = ((bf16[3,8,128,256]{2,3,0,1:T(8,128)(2,1)}), bf16[3,8,128,256]{2,3,0,1:T(8,128)(2,1)S(1)}, u32[]{:S(2)}, u32[]{:S(2)}) async-start(bf16[3,8,128,256]{2,3,0,1:T(8,128)(2,1)} %pad_maximum_fusion.1), calls=%async_computation.1 | async-start | bytes 3145728 | tf_op jit(solution)/shard_map/all_to_all | solution.py:151
  117.0 1.5 fusion.70
  118.5 1.2 copy.98
  119.8 1.1 copy.99
  120.9 5.9 %convert_reduce_fusion = bf16[256,2048]{1,0:T(8,128)(2,1)} fusion(bf16[8,128,2048]{2,1,0:T(8,128)(2,1)} %bitcast.122, bf16[32,8,8,128]{3,2,1,0:T(8,128)(2,1)} %get-tuple-element.26), kind=kOutput, calls=%fused_computation | convolution fusion | flops 1081606144 | bytes 5767168 | tf_op jit(solution)/shard_map/bnf,bnk->bfk/dot_general | solution.py:126
  126.8 1.4 reshape.64
  128.2 0.7 fusion.71
  128.9 0.5 copy.100
  129.4 0.5 copy.101
  130.0 4.7 %fusion.74 = (bf16[4,128,2048]{2,1,0:T(8,128)(2,1)S(1)}, f32[4,128,2048]{2,1,0:T(8,128)}) fusion(bf16[256,2048]{1,0:T(8,128)(2,1)} %collective-permute-done.1, bf16[256,2048]{1,0:T(8,128)(2,1)} %param.11, bf16[4,128,256]{2,1,0:T(8,128)(2,1)S(1)} %get-tuple-element.39, bf16[4,128,256]{2,1,0:T(8,128)(2,1)S(1)} %get-tuple-element.40), kind=kOutput, calls=%fused_computation.99 | convolution fusion | flops 1080033280 | bytes 8912896 | tf_op jit(solution)/shard_map/dot_general | solution.py:67
  134.9 1.5 collective-permute-start.2
  136.4 1.0 collective-permute-start.3
  137.5 1.9 collective-permute-start.4
  139.4 41.1 %all-reduce.2.cloned.1.call-done = bf16[256,2048]{1,0:T(8,128)(2,1)} async-done(((bf16[256,2048]{1,0:T(8,128)(2,1)}), bf16[256,2048]{1,0:T(8,128)(2,1)}) %all-reduce.2.cloned.1.call-update) | async-done | bytes 1048592 | tf_op jit(solution)/shard_map/psum | solution.py:130
  180.4 2.8 %convert_multiply_fusion = f32[256,2048]{1,0:T(8,128)} fusion(bf16[256,2048]{1,0:T(8,128)(2,1)} %all-reduce.2.cloned.1.call-done), kind=kLoop, calls=%fused_computation.23 | loop fusion | flops 1048576 | bytes 3145728 | tf_op jit(solution)/shard_map/div | solution.py:132
  183.2 1.9 collective-permute-done.2
  185.1 11.2 %collective-permute-done.3 = bf16[128,2048]{1,0:T(8,128)(2,1)} collective-permute-done((bf16[128,2048]{1,0:T(8,128)(2,1)S(1)}, bf16[128,2048]{1,0:T(8,128)(2,1)}, u32[]{:S(2)}, u32[]{:S(2)}) %collective-permute-start.3) | collective-permute-done | bytes 524320 | tf_op jit(solution)/shard_map/ppermute | solution.py:75
  196.3 2.2 %collective-permute-done.4 = bf16[128,2048]{1,0:T(8,128)(2,1)} collective-permute-done((bf16[128,2048]{1,0:T(8,128)(2,1)S(1)}, bf16[128,2048]{1,0:T(8,128)(2,1)}, u32[]{:S(2)}, u32[]{:S(2)}) %collective-permute-start.4) | collective-permute-done | bytes 524320 | tf_op jit(solution)/shard_map/ppermute | solution.py:75
  198.5 2.8 %fusion.42 = bf16[1,128,2048]{2,1,0:T(8,128)(2,1)} fusion(bf16[128,2048]{1,0:T(8,128)(2,1)} %collective-permute-done.4, bf16[128,2048]{1,0:T(8,128)(2,1)} %collective-permute-done.3, bf16[128,2048]{1,0:T(8,128)(2,1)} %collective-permute-done.2, f32[4,128,2048]{2,1,0:T(8,128)} %get-tuple-element.37, s32[]{:T(128)S(6)} %select_n.72), kind=kLoop, calls=%fused_computation.49 | loop fusion | flops 1835008 | bytes 3145732 | tf_op jit(solution)/shard_map/broadcast_in_dim | solution.py:120
  201.4 1.0 copy.90
  202.4 1.0 copy.91
  203.4 1.0 copy.92
  (44 shorter events, 3.6 us)
Async XLA Ops:
  7.2 86.7 %all-gather.3.cloned.1.call-start = ((), (), s32[]{:S(2)}) async-start(), calls=%async_computation.3 | async-start | bytes 4718592 | tf_op jit(solution)/shard_map/all_gather | solution.py:93
  11.9 6.9 %copy-start.4 = (s32[1,9]{1,0:T(1,128)S(1)}, s32[1,9]{1,0:T(1,128)}, u32[]{:S(2)}) copy-start(s32[1,9]{1,0:T(1,128)} %param.12) | copy-start | bytes 112
  11.9 7.1 %copy-start.5 = (s32[1,32]{1,0:T(1,128)S(1)}, s32[1,32]{1,0:T(1,128)}, u32[]{:S(2)}) copy-start(s32[1,32]{1,0:T(1,128)} %param.13) | copy-start | bytes 388
  13.3 73.4 %all-to-all-start = ((bf16[3,8,128,256]{2,3,0,1:T(8,128)(2,1)}), bf16[3,8,128,256]{2,3,0,1:T(8,128)(2,1)S(1)}, u32[]{:S(2)}, u32[]{:S(2)}) async-start(bf16[3,8,128,256]{2,3,0,1:T(8,128)(2,1)} %copy.75), calls=%async_computation | async-start | bytes 3145728 | tf_op jit(solution)/shard_map/all_to_all | solution.py:108
  18.6 111.3 %collective-permute-start.1 = (bf16[256,2048]{1,0:T(8,128)(2,1)}, bf16[256,2048]{1,0:T(8,128)(2,1)}, u32[]{:S(2)}, u32[]{:S(2)}) collective-permute-start(bf16[256,2048]{1,0:T(8,128)(2,1)} %param.11), channel_id=1, source_target_pairs={{0,1},{1,0},{2,3},{3,2},{4,5},{5,4},{6,7},{7,6},{8,9},{9,8},{10,11... | collective-permute-start | bytes 3145736 | tf_op jit(solution)/shard_map/ppermute | solution.py:59
  89.1 2.0 copy-start
  91.1 2.0 copy-start.2
  93.9 3.9 %copy-start.1 = (f32[1024,1024]{0,1:T(8,128)S(1)}, f32[1024,1024]{0,1:T(8,128)}, u32[]{:S(2)}) copy-start(f32[1024,1024]{0,1:T(8,128)} %copy-done) | copy-start | bytes 12582916
  99.9 2.2 %copy-start.3 = (f32[1024,1024]{0,1:T(8,128)S(1)}, f32[1024,1024]{0,1:T(8,128)}, u32[]{:S(2)}) copy-start(f32[1024,1024]{0,1:T(8,128)} %copy-done.2) | copy-start | bytes 12582916
  107.6 19.1 %collective-permute-start = (bf16[1024,256]{0,1:T(8,128)(2,1)S(1)}, bf16[1024,256]{0,1:T(8,128)(2,1)}, u32[]{:S(2)}, u32[]{:S(2)}) collective-permute-start(bf16[1024,256]{0,1:T(8,128)(2,1)S(1)} %get-tuple-element.27), channel_id=1, source_target_pairs={{0,1},{1,0},{2,3},{3,2},{4,5},{5,4},{6,7},{7,6},{8,9},{9,8},{10,11... | collective-permute-start | bytes 1572872 | tf_op jit(solution)/shard_map/ppermute | solution.py:58
  110.1 91.2 %all-to-all-start.1 = ((bf16[3,8,128,256]{2,3,0,1:T(8,128)(2,1)}), bf16[3,8,128,256]{2,3,0,1:T(8,128)(2,1)S(1)}, u32[]{:S(2)}, u32[]{:S(2)}) async-start(bf16[3,8,128,256]{2,3,0,1:T(8,128)(2,1)} %pad_maximum_fusion.1), calls=%async_computation.1 | async-start | bytes 3145728 | tf_op jit(solution)/shard_map/all_to_all | solution.py:151
  117.0 63.4 %all-reduce.2.cloned.1.call-start = ((), (), s32[]{:S(2)}) async-start(), calls=%async_computation.2 | async-start | bytes 2097152 | tf_op jit(solution)/shard_map/psum | solution.py:130
  134.9 50.2 %collective-permute-start.2 = (bf16[128,2048]{1,0:T(8,128)(2,1)S(1)}, bf16[128,2048]{1,0:T(8,128)(2,1)}, u32[]{:S(2)}, u32[]{:S(2)}) collective-permute-start(bf16[128,2048]{1,0:T(8,128)(2,1)S(1)} %get-tuple-element.17), channel_id=1, source_target_pairs={{0,2},{1,3},{2,4},{3,5},{4,6},{5,7},{6,0},{7,1},{8,10},{9,11},{10,... | collective-permute-start | bytes 1572872 | tf_op jit(solution)/shard_map/ppermute | solution.py:75
  136.4 59.8 %collective-permute-start.3 = (bf16[128,2048]{1,0:T(8,128)(2,1)S(1)}, bf16[128,2048]{1,0:T(8,128)(2,1)}, u32[]{:S(2)}, u32[]{:S(2)}) collective-permute-start(bf16[128,2048]{1,0:T(8,128)(2,1)S(1)} %get-tuple-element.19), channel_id=1, source_target_pairs={{0,4},{1,5},{2,6},{3,7},{4,0},{5,1},{6,2},{7,3},{8,12},{9,13},{10,... | collective-permute-start | bytes 1572872 | tf_op jit(solution)/shard_map/ppermute | solution.py:75
  137.5 61.0 %collective-permute-start.4 = (bf16[128,2048]{1,0:T(8,128)(2,1)S(1)}, bf16[128,2048]{1,0:T(8,128)(2,1)}, u32[]{:S(2)}, u32[]{:S(2)}) collective-permute-start(bf16[128,2048]{1,0:T(8,128)(2,1)S(1)} %get-tuple-element.18), channel_id=1, source_target_pairs={{0,6},{1,7},{2,0},{3,1},{4,2},{5,3},{6,4},{7,5},{8,14},{9,15},{10,... | collective-permute-start | bytes 1572872 | tf_op jit(solution)/shard_map/ppermute | solution.py:75
Sparse Core Ops, SparseCore 0:
  9.6 77.0 all-gather.2
  126.9 53.4 all-reduce.1
where the time goes:
time: 212 us; the launch traced here: 211 us
  waiting for transfers between devices  124 us (58%)
  matrix products  25.9 us (12%)
  local copies, waits for them, and re-layouts  19.9 us (9%)
  starting transfers between devices  17 us (8%)
  between operations  14.4 us (7%)
  other arithmetic  9.61 us (5%)
    all_to_all x1, waiting for transfers between devices, shards(): lax.all_to_all(stacked, 'seq', split_axis=1, concat_axis=1, tiled=True)  67.4 us
    psum x1, waiting for transfers between devices, shards(): w_rows = lax.psum(w_rows.astype(jnp.bfloat16), 'dp').astype(jnp.float32)  41.1 us
    ppermute x3, waiting for transfers between devices, chip_layer_out(): total = total + lax.ppermute(piece, 'seq', pairs).astype(jnp.float32)  15.3 us
    unnamed x28, local copies, waits for them, and re-layouts  13.5 us
    all_to_all x1, starting transfers between devices, shards(): back = lax.all_to_all(grads, 'seq', split_axis=1, concat_axis=1, tiled=True)  6.9 us
    dot_general x1, matrix products, shards(): jnp.einsum('bnf,bnk->bfk', att_blocks, grad_blocks, preferred_element_typ...  5.87 us
    all_to_all x1, starting transfers between devices, shards(): lax.all_to_all(stacked, 'seq', split_axis=1, concat_axis=1, tiled=True)  5.32 us
    dot_general x1, matrix products, chip_layer_out(): lax.dot_general(att_chip, w_chip, (((2,), (0,)), ((), ())), preferred_ele...  4.73 us
  transfers between devices with their start and end apart: 9, of which 5 were waited for; matrix products, arithmetic and copies ran while one was open for 24% of the time, Pallas kernels for 0%

commit v1 on v0

--- a/solution.py
+++ b/solution.py
@@ -6,6 +6,11 @@
 
 H = 16
 HD = 128
+
+
+def gather_and_add(value, name):
+    parts = lax.all_gather(value, name)
+    return jnp.sum(parts, axis=0)
 
 
 def tile_mask(starts, columns, nodes):
@@ -127,7 +132,7 @@
         "bnf,bnk->bfk", att_blocks, grad_blocks, preferred_element_type=jnp.float32
     ).astype(jnp.bfloat16)
     w_rows = jnp.sum(terms.astype(jnp.float32), axis=0)
-    w_rows = lax.psum(w_rows.astype(jnp.bfloat16), "dp").astype(jnp.float32)
+    w_rows = gather_and_add(w_rows.astype(jnp.bfloat16), "dp").astype(jnp.float32)
     batch = asking_vectors_matrix.shape[0] * lax.axis_size("dp")
     w_out_grad = w_rows / batch
     bwd = [

time: 212 us -> 222 us (1.047)
  waiting for transfers between devices: 124 us -> 132 us
    ppermute x3, waiting for transfers between devices: 15.3 us -> 64.1 us  [chip_layer_out(): total = total + lax.ppermute(piece, 'seq', pairs).astype(jnp.float32)]
    psum x1 -> x0, waiting for transfers between devices: 41.1 us -> none  [shards(): w_rows = lax.psum(w_rows.astype(jnp.bfloat16), 'dp').astype(jnp.float32)]
    reduce_sum x0 -> x1, other arithmetic: none -> 3.07 us  [gather_and_add(): return jnp.sum(parts, axis=0)]
    dot_general x1, matrix products: 5.87 us -> 3.41 us  [shards(): jnp.einsum('bnf,bnk->bfk', att_blocks, grad_blocks, preferred_element_typ...]
    dot_general x2, matrix products: 2.39 us -> 4.75 us  [attend_back(): prob_grad = jnp.dot(g, v.T, preferred_element_type=jnp.float32)]
    unnamed x28 -> x32, local copies, waits for them, and re-layouts: 13.5 us -> 14.1 us
  transfers between devices with their start and end apart: 9 -> 9, of which waited for: 5 -> 4; matrix products, arithmetic and copies ran while one was open for 24% -> 19% of each run, Pallas kernels for 0% -> 0%
where the time goes in v1:
time: 222 us
  waiting for transfers between devices  132 us (59%)
  matrix products  25.9 us (12%)
  local copies, waits for them, and re-layouts  20.5 us (9%)
  starting transfers between devices  17.7 us (8%)
  between operations  14.5 us (7%)
  other arithmetic  10.6 us (5%)
    all_to_all x1, waiting for transfers between devices, shards(): lax.all_to_all(stacked, 'seq', split_axis=1, concat_axis=1, tiled=True)  67.6 us
    ppermute x3, waiting for transfers between devices, chip_layer_out(): total = total + lax.ppermute(piece, 'seq', pairs).astype(jnp.float32)  64.1 us
    unnamed x32, local copies, waits for them, and re-layouts  14.1 us
    all_to_all x1, starting transfers between devices, shards(): back = lax.all_to_all(grads, 'seq', split_axis=1, concat_axis=1, tiled=True)  7.36 us
    all_to_all x1, starting transfers between devices, shards(): lax.all_to_all(stacked, 'seq', split_axis=1, concat_axis=1, tiled=True)  5.32 us
    dot_general x1, matrix products, chip_layer_out(): lax.dot_general(att_chip, w_chip, (((2,), (0,)), ((), ())), preferred_ele...  4.79 us
    dot_general x2, matrix products, attend_back(): prob_grad = jnp.dot(g, v.T, preferred_element_type=jnp.float32)  4.75 us
    ppermute x3, starting transfers between devices, chip_layer_out(): total = total + lax.ppermute(piece, 'seq', pairs).astype(jnp.float32)  4.47 us
  transfers between devices with their start and end apart: 9, of which 4 were waited for; matrix products, arithmetic and copies ran while one was open for 19% of the time, Pallas kernels for 0%

profile of v1, /device:TPU:10, one launch (start us, length us, event | category | flops | bytes accessed | tf_op | source)
XLA Modules:
  0.0 221.5 jit_solution(17956990054674170533)
XLA Ops:
  7.2 0.7 all-gather.5.cloned.1.call-update
  7.9 1.3 copy.72
  9.2 1.3 copy.73
  10.5 1.3 copy.74
  12.1 1.2 copy.75
  13.3 5.3 %all-to-all-start = ((bf16[3,8,128,256]{2,3,0,1:T(8,128)(2,1)}), bf16[3,8,128,256]{2,3,0,1:T(8,128)(2,1)S(1)}, u32[]{:S(2)}, u32[]{:S(2)}) async-start(bf16[3,8,128,256]{2,3,0,1:T(8,128)(2,1)} %copy.75), calls=%async_computation | async-start | bytes 3145728 | tf_op jit(solution)/shard_map/all_to_all | solution.py:113
  19.1 67.6 %all-to-all-done = bf16[3,8,128,256]{2,3,0,1:T(8,128)(2,1)S(1)} async-done(((bf16[3,8,128,256]{2,3,0,1:T(8,128)(2,1)}), bf16[3,8,128,256]{2,3,0,1:T(8,128)(2,1)S(1)}, u32[]{:S(2)}, u32[]{:S(2)}) %all-to-all-start) | async-done | bytes 1572896 | tf_op jit(solution)/shard_map/all_to_all | solution.py:113
  87.8 1.2 fusion.73
  89.1 0.6 fusion.2
  89.7 1.2 fusion.72
  91.0 0.6 fusion.4
  91.7 1.3 copy-done.3
  93.0 0.8 fusion.32
  93.9 3.9 %fusion.21 = bf16[1024,256]{0,1:T(8,128)(2,1)S(1)} fusion(bf16[256,2048]{1,0:T(8,128)(2,1)} %param.11, bf16[1,1024,2048]{2,1,0:T(8,128)(2,1)} %all-gather.5.cloned.1.call-done), kind=kOutput, calls=%fused_computation.32 | convolution fusion | flops 1074003968 | bytes 5767168 | tf_op jit(solution)/shard_map/dot_general | solution.py:126
  97.8 0.9 multiply_reduce_fusion.1
  98.8 1.2 copy-done.5
  100.0 3.4 %convert_reduce_fusion = bf16[256,2048]{1,0:T(8,128)(2,1)} fusion(bf16[8,128,2048]{2,1,0:T(8,128)(2,1)S(1)} %bitcast.124, bf16[32,8,8,128]{3,2,1,0:T(8,128)(2,1)S(1)} %get-tuple-element.26), kind=kOutput, calls=%fused_computation | convolution fusion | flops 1081606144 | bytes 5767168 | tf_op jit(solution)/shard_map/bnf,bnk->bfk/dot_general | solution.py:131
  103.5 3.5 %multiply_convert_fusion.1 = bf16[1024,1024]{0,1:T(8,128)(2,1)S(1)} fusion(f32[1024,1024]{0,1:T(8,128)} %copy-done, f32[1024]{0:T(1024)S(1)} %get-tuple-element.15, f32[1024]{0:T(1024)S(1)} %broadcast_divide_fusion.1, f32[1024]{0:T(1024)S(1)} %get-tuple-element.34, bf16[1024,256]{1,0:T(8,128)(2,1)S(1)} %bitcast.122, bf16[1024,256]{0,1:T(8,128)(2,1)S(1)} %fusion.21), kind=kOutput, calls=%fused_computation.6 | convolution fusion | flops 274726912 | bytes 6828032 | tf_op jit(solution)/shard_map/dot_general | solution.py:47
  107.0 0.5 convolution_convert_fusion.3
  107.5 1.2 multiply_convert_fusion
  108.7 0.7 convolution_convert_fusion.2
  109.7 0.8 convolution_convert_fusion.1
  110.5 0.8 convolution_convert_fusion
  111.8 0.9 fusion.31
  112.8 0.9 fusion.30
  114.0 1.3 pad_maximum_fusion.1
  115.3 7.4 %all-to-all-start.1 = ((bf16[3,8,128,256]{2,3,0,1:T(8,128)(2,1)}), bf16[3,8,128,256]{2,3,0,1:T(8,128)(2,1)S(1)}, u32[]{:S(2)}, u32[]{:S(2)}) async-start(bf16[3,8,128,256]{2,3,0,1:T(8,128)(2,1)} %pad_maximum_fusion.1), calls=%async_computation.1 | async-start | bytes 3145728 | tf_op jit(solution)/shard_map/all_to_all | solution.py:156
  123.1 0.4 reshape.63
  123.5 1.5 fusion.70
  125.0 1.2 copy.98
  126.3 1.1 copy.99
  127.4 1.4 reshape.64
  128.8 0.7 fusion.71
  129.5 0.5 copy.100
  130.0 0.5 copy.101
  130.6 4.8 %fusion.74 = (bf16[4,128,2048]{2,1,0:T(8,128)(2,1)S(1)}, f32[4,128,2048]{2,1,0:T(8,128)}) fusion(bf16[256,2048]{1,0:T(8,128)(2,1)} %collective-permute-done.1, bf16[256,2048]{1,0:T(8,128)(2,1)} %param.11, bf16[4,128,256]{2,1,0:T(8,128)(2,1)S(1)} %get-tuple-element.39, bf16[4,128,256]{2,1,0:T(8,128)(2,1)S(1)} %get-tuple-element.40), kind=kOutput, calls=%fused_computation.99 | convolution fusion | flops 1080033280 | bytes 8912896 | tf_op jit(solution)/shard_map/dot_general | solution.py:72
  135.5 1.5 collective-permute-start.2
  137.1 1.1 collective-permute-start.3
  138.1 1.9 collective-permute-start.4
  140.0 50.7 %collective-permute-done.2 = bf16[128,2048]{1,0:T(8,128)(2,1)} collective-permute-done((bf16[128,2048]{1,0:T(8,128)(2,1)S(1)}, bf16[128,2048]{1,0:T(8,128)(2,1)}, u32[]{:S(2)}, u32[]{:S(2)}) %collective-permute-start.2) | collective-permute-done | bytes 524320 | tf_op jit(solution)/shard_map/ppermute | solution.py:80
  190.7 11.2 %collective-permute-done.3 = bf16[128,2048]{1,0:T(8,128)(2,1)} collective-permute-done((bf16[128,2048]{1,0:T(8,128)(2,1)S(1)}, bf16[128,2048]{1,0:T(8,128)(2,1)}, u32[]{:S(2)}, u32[]{:S(2)}) %collective-permute-start.3) | collective-permute-done | bytes 524320 | tf_op jit(solution)/shard_map/ppermute | solution.py:80
  201.9 2.2 %collective-permute-done.4 = bf16[128,2048]{1,0:T(8,128)(2,1)} collective-permute-done((bf16[128,2048]{1,0:T(8,128)(2,1)S(1)}, bf16[128,2048]{1,0:T(8,128)(2,1)}, u32[]{:S(2)}, u32[]{:S(2)}) %collective-permute-start.4) | collective-permute-done | bytes 524320 | tf_op jit(solution)/shard_map/ppermute | solution.py:80
  204.1 2.8 %fusion.42 = bf16[1,128,2048]{2,1,0:T(8,128)(2,1)} fusion(bf16[128,2048]{1,0:T(8,128)(2,1)} %collective-permute-done.4, bf16[128,2048]{1,0:T(8,128)(2,1)} %collective-permute-done.3, bf16[128,2048]{1,0:T(8,128)(2,1)} %collective-permute-done.2, f32[4,128,2048]{2,1,0:T(8,128)} %get-tuple-element.37, s32[]{:T(128)S(6)} %select_n.72), kind=kLoop, calls=%fused_computation.49 | loop fusion | flops 1835008 | bytes 3145732 | tf_op jit(solution)/shard_map/broadcast_in_dim | solution.py:125
  207.0 1.0 copy.90
  208.0 1.0 copy.91
  209.0 1.0 copy.92
  210.1 3.1 %reduce_sum.75 = bf16[256,2048]{1,0:T(8,128)(2,1)S(1)} reduce(bf16[4,256,2048]{2,1,0:T(8,128)(2,1)} %bitcast.106, bf16[]{:T(256)} %constant.74.clone.1), dimensions={0}, to_apply=%region_8.9 | reduce | flops 1572864 | bytes 5242882 | tf_op jit(solution)/shard_map/reduce_sum | solution.py:13
  213.1 1.6 convert_multiply_fusion
  (49 shorter events, 3.9 us)
Async XLA Ops:
  7.2 86.7 %all-gather.5.cloned.1.call-start = ((), (), s32[]{:S(2)}) async-start(), calls=%async_computation.2 | async-start | bytes 4718592 | tf_op jit(solution)/shard_map/all_gather | solution.py:98
  11.9 6.8 %copy-start.6 = (s32[1,9]{1,0:T(1,128)S(1)}, s32[1,9]{1,0:T(1,128)}, u32[]{:S(2)}) copy-start(s32[1,9]{1,0:T(1,128)} %param.12) | copy-start | bytes 112
  11.9 6.9 %copy-start.7 = (s32[1,32]{1,0:T(1,128)S(1)}, s32[1,32]{1,0:T(1,128)}, u32[]{:S(2)}) copy-start(s32[1,32]{1,0:T(1,128)} %param.13) | copy-start | bytes 388
  13.3 73.4 %all-to-all-start = ((bf16[3,8,128,256]{2,3,0,1:T(8,128)(2,1)}), bf16[3,8,128,256]{2,3,0,1:T(8,128)(2,1)S(1)}, u32[]{:S(2)}, u32[]{:S(2)}) async-start(bf16[3,8,128,256]{2,3,0,1:T(8,128)(2,1)} %copy.75), calls=%async_computation | async-start | bytes 3145728 | tf_op jit(solution)/shard_map/all_to_all | solution.py:113
  18.6 191.4 %all-gather.7.cloned.1.call-start = ((), (), s32[]{:S(2)}) async-start(), calls=%async_computation.3 | async-start | bytes 5242880 | tf_op jit(solution)/shard_map/all_gather | solution.py:12
  89.1 2.0 copy-start
  91.0 2.0 copy-start.3
  93.9 3.9 %copy-start.1 = (f32[1024,1024]{0,1:T(8,128)S(1)}, f32[1024,1024]{0,1:T(8,128)}, u32[]{:S(2)}) copy-start(f32[1024,1024]{0,1:T(8,128)} %copy-done) | copy-start | bytes 12582916
  97.8 2.2 copy-start.5
  103.4 4.1 %copy-start.4 = (f32[1024,1024]{0,1:T(8,128)S(1)}, f32[1024,1024]{0,1:T(8,128)}, u32[]{:S(2)}) copy-start(f32[1024,1024]{0,1:T(8,128)} %copy-done.3) | copy-start | bytes 12582916
  109.7 2.2 copy-start.2
  115.3 91.6 %all-to-all-start.1 = ((bf16[3,8,128,256]{2,3,0,1:T(8,128)(2,1)}), bf16[3,8,128,256]{2,3,0,1:T(8,128)(2,1)S(1)}, u32[]{:S(2)}, u32[]{:S(2)}) async-start(bf16[3,8,128,256]{2,3,0,1:T(8,128)(2,1)} %pad_maximum_fusion.1), calls=%async_computation.1 | async-start | bytes 3145728 | tf_op jit(solution)/shard_map/all_to_all | solution.py:156
  122.6 4.8 %collective-permute-start = (bf16[1024,256]{0,1:T(8,128)(2,1)S(1)}, bf16[1024,256]{0,1:T(8,128)(2,1)}, u32[]{:S(2)}, u32[]{:S(2)}) collective-permute-start(bf16[1024,256]{0,1:T(8,128)(2,1)S(1)} %get-tuple-element.27), channel_id=1, source_target_pairs={{0,1},{1,0},{2,3},{3,2},{4,5},{5,4},{6,7},{7,6},{8,9},{9,8},{10,11... | collective-permute-start | bytes 1572872 | tf_op jit(solution)/shard_map/ppermute | solution.py:63
  122.8 7.8 %collective-permute-start.1 = (bf16[256,2048]{1,0:T(8,128)(2,1)}, bf16[256,2048]{1,0:T(8,128)(2,1)}, u32[]{:S(2)}, u32[]{:S(2)}) collective-permute-start(bf16[256,2048]{1,0:T(8,128)(2,1)} %param.11), channel_id=1, source_target_pairs={{0,1},{1,0},{2,3},{3,2},{4,5},{5,4},{6,7},{7,6},{8,9},{9,8},{10,11... | collective-permute-start | bytes 3145736 | tf_op jit(solution)/shard_map/ppermute | solution.py:64
  135.5 55.1 %collective-permute-start.2 = (bf16[128,2048]{1,0:T(8,128)(2,1)S(1)}, bf16[128,2048]{1,0:T(8,128)(2,1)}, u32[]{:S(2)}, u32[]{:S(2)}) collective-permute-start(bf16[128,2048]{1,0:T(8,128)(2,1)S(1)} %get-tuple-element.17), channel_id=1, source_target_pairs={{0,2},{1,3},{2,4},{3,5},{4,6},{5,7},{6,0},{7,1},{8,10},{9,11},{10,... | collective-permute-start | bytes 1572872 | tf_op jit(solution)/shard_map/ppermute | solution.py:80
  137.1 64.8 %collective-permute-start.3 = (bf16[128,2048]{1,0:T(8,128)(2,1)S(1)}, bf16[128,2048]{1,0:T(8,128)(2,1)}, u32[]{:S(2)}, u32[]{:S(2)}) collective-permute-start(bf16[128,2048]{1,0:T(8,128)(2,1)S(1)} %get-tuple-element.19), channel_id=1, source_target_pairs={{0,4},{1,5},{2,6},{3,7},{4,0},{5,1},{6,2},{7,3},{8,12},{9,13},{10,... | collective-permute-start | bytes 1572872 | tf_op jit(solution)/shard_map/ppermute | solution.py:80
  138.1 66.0 %collective-permute-start.4 = (bf16[128,2048]{1,0:T(8,128)(2,1)S(1)}, bf16[128,2048]{1,0:T(8,128)(2,1)}, u32[]{:S(2)}, u32[]{:S(2)}) collective-permute-start(bf16[128,2048]{1,0:T(8,128)(2,1)S(1)} %get-tuple-element.18), channel_id=1, source_target_pairs={{0,6},{1,7},{2,0},{3,1},{4,2},{5,3},{6,4},{7,5},{8,14},{9,15},{10,... | collective-permute-start | bytes 1572872 | tf_op jit(solution)/shard_map/ppermute | solution.py:80
Sparse Core Ops, SparseCore 0:
  9.6 77.0 all-gather.4
  103.5 54.5 all-gather.6
